TPU v7x, 512 devices: a whole 4x4x16 slice. The times are simulated.
512 devices in a mesh: ctx: 32 (over z, core), uly: 16 (over x, y).
Axes of the slice: x: 4, y: 4, z: 16, core: 2. Of those that a mesh axis runs over, the one named last changes fastest.
Arguments:
- query_heads: bfloat16 [1, 8192, 8192], P(None, 'ctx', 'uly'), may hold values from -2.5 to 2.5
- key_heads: bfloat16 [1, 8192, 8192], P(None, 'ctx', 'uly'), may hold values from -2.5 to 2.5
- value_heads: bfloat16 [1, 8192, 8192], P(None, 'ctx', 'uly'), may hold values from -2.5 to 2.5
- grad_out: bfloat16 [1, 8192, 8192], P(None, ('ctx', 'uly')), may hold values from -2.5 to 2.5
- log_decay: float32 [1, 64, 8192], P(None, 'uly', 'ctx'), as said below
Outputs:
- attended: bfloat16 [1, 8192, 8192], P(None, ('ctx', 'uly'))
- grad_query: bfloat16 [1, 8192, 8192], P(None, ('ctx', 'uly'))
- grad_key: bfloat16 [1, 8192, 8192], P(None, ('ctx', 'uly'))
- grad_value: bfloat16 [1, 8192, 8192], P(None, ('ctx', 'uly'))
Inputs may be any that keep to these rules, and one draw needn't show every extreme that they name: `log_decay`: each entry is the logarithm of the share of a head's state that the position keeps.
All inputs are finite; a program needn't handle non-finite values.
Results may differ from a plain program's by a relative error of at most 0.0063.
Values may be sent and summed in bfloat16 or wider, within the bound.
No kernel may reach another device: no remote copies, remote signals or barrier semaphores. Data moves between devices by JAX's collectives and lax.ppermute only.
A program may use at most 64 MiB of HBM per device.

v0:
```python
import jax
import jax.numpy as jnp
from jax import lax
from jax.sharding import PartitionSpec as P


def entering(value, axis, join, neutral, backward):
    count, mine = (lax.axis_size(axis), lax.axis_index(axis))
    pieces = jax.tree.map(lambda part: lax.all_gather(part, axis), value)
    if backward:
        pieces = jax.tree.map(lambda part: part[::-1], pieces)
        mine = count - 1 - mine
    so_far = jax.tree.map(
        lambda part, zero: jnp.full_like(part, 0) + jnp.asarray(zero, part.dtype), value, neutral
    )

    def hop(position, so_far):
        longer = join(so_far, jax.tree.map(lambda part: part[position], pieces))
        return jax.tree.map(lambda new, old: jnp.where(position < mine, new, old), longer, so_far)

    return lax.fori_loop(0, count - 1, hop, so_far)


def decay_tables(log_decay):
    cumulative = jnp.cumsum(log_decay, axis=-1)
    last_cum = cumulative[..., -1:]
    block_len = log_decay.shape[-1]
    row_ids = lax.broadcasted_iota(jnp.int32, (block_len, block_len), 0)
    col_ids = lax.broadcasted_iota(jnp.int32, (block_len, block_len), 1)
    lower_tri = row_ids >= col_ids
    spread = cumulative[..., :, None] - cumulative[..., None, :]
    decay_mask = jnp.where(lower_tri, jnp.exp(jnp.where(lower_tri, spread, 0.0)), 0.0)
    return (cumulative, last_cum, decay_mask)


def to_rows(table):
    return jnp.swapaxes(table, 1, 2)[..., None]


def combine(earlier, latter):
    return (earlier[0] * latter[0], latter[0][..., None, None] * earlier[1] + latter[1])


def local(query_heads, key_heads, value_heads, grad_out, log_decay):
    batch_count, positions, width_all = query_heads.shape
    head_count = log_decay.shape[1]
    head_shape = (batch_count, positions, head_count, width_all // head_count)
    q_split = query_heads.reshape(head_shape)
    k_split = key_heads.reshape(head_shape)
    v_split = value_heads.reshape(head_shape)
    incoming = lax.all_to_all(grad_out, "uly", split_axis=2, concat_axis=1, tiled=True)
    g_split = incoming.reshape(head_shape)
    cumulative, last_cum, decay_mask = decay_tables(log_decay)
    block_keep = jnp.exp(last_cum[..., 0])
    rise_rows = to_rows(jnp.exp(cumulative))
    fall_rows = to_rows(jnp.exp(last_cum - cumulative))
    scaled_query = (rise_rows * q_split).astype(jnp.bfloat16)
    scaled_key = (fall_rows * k_split).astype(jnp.bfloat16)
    update = jnp.einsum("bjhd,bjhe->bhde", scaled_key, v_split, preferred_element_type=jnp.float32)
    local_grad = jnp.einsum(
        "bihd,bihe->bhde", scaled_query, g_split, preferred_element_type=jnp.float32
    )
    state_in = entering(
        (block_keep, update),
        "ctx",
        combine,
        (jnp.ones_like(block_keep), jnp.zeros_like(update)),
        False,
    )[1]
    carried = entering(
        (block_keep, local_grad),
        "ctx",
        combine,
        (jnp.ones_like(block_keep), jnp.zeros_like(local_grad)),
        True,
    )[1]
    scores = jnp.einsum("bihd,bjhd->bhij", q_split, k_split, preferred_element_type=jnp.float32)
    attn_weights = (scores * decay_mask).astype(jnp.bfloat16)
    grad_raw = jnp.einsum("bihe,bjhe->bhij", g_split, v_split, preferred_element_type=jnp.float32)
    grad_scores = (grad_raw * decay_mask).astype(jnp.bfloat16)
    state_b = state_in.astype(jnp.bfloat16)
    attended = jnp.einsum(
        "bhij,bjhd->bihd", attn_weights, v_split, preferred_element_type=jnp.float32
    )
    attended = attended + jnp.einsum(
        "bihd,bhde->bihe", scaled_query, state_b, preferred_element_type=jnp.float32
    )
    query_part = jnp.einsum(
        "bhij,bjhd->bihd", grad_scores, k_split, preferred_element_type=jnp.float32
    )
    query_part = query_part + rise_rows * jnp.einsum(
        "bihe,bhde->bihd", g_split, state_b, preferred_element_type=jnp.float32
    )
    carried_b = carried.astype(jnp.bfloat16)
    key_part = jnp.einsum(
        "bhij,bihd->bjhd", grad_scores, q_split, preferred_element_type=jnp.float32
    )
    key_part = key_part + fall_rows * jnp.einsum(
        "bjhe,bhde->bjhd", v_split, carried_b, preferred_element_type=jnp.float32
    )
    value_part = jnp.einsum(
        "bhij,bihe->bjhe", attn_weights, g_split, preferred_element_type=jnp.float32
    )
    value_part = value_part + fall_rows * jnp.einsum(
        "bjhd,bhde->bjhe", k_split, carried_b, preferred_element_type=jnp.float32
    )

    def to_tokens(array):
        return array.astype(jnp.bfloat16).reshape(batch_count, positions, width_all)

    attended_rows, query_rows, key_rows, value_rows = (
        lax.all_to_all(to_tokens(attended), "uly", split_axis=1, concat_axis=2, tiled=True),
        lax.all_to_all(to_tokens(query_part), "uly", split_axis=1, concat_axis=2, tiled=True),
        lax.all_to_all(to_tokens(key_part), "uly", split_axis=1, concat_axis=2, tiled=True),
        lax.all_to_all(to_tokens(value_part), "uly", split_axis=1, concat_axis=2, tiled=True),
    )
    return (attended_rows, query_rows, key_rows, value_rows)


def solution(mesh):
    placed = (
        P(None, "ctx", "uly"),
        P(None, "ctx", "uly"),
        P(None, "ctx", "uly"),
        P(None, ("ctx", "uly"), None),
        P(None, "uly", "ctx"),
    )
    return jax.shard_map(
        local,
        mesh=mesh,
        in_specs=placed,
        out_specs=(
            P(None, ("ctx", "uly"), None),
            P(None, ("ctx", "uly"), None),
            P(None, ("ctx", "uly"), None),
            P(None, ("ctx", "uly"), None),
        ),
        check_vma=False,
    )
```

profile of v0, /device:TPU:8, one launch (start us, length us, event | category | flops | bytes accessed | tf_op | source)
XLA Modules:
  0.0 278.4 jit_solution(11245880832409896783)
XLA Ops:
  7.9 1.2 reduce-window.6
  9.5 1.1 reshape.285
  12.9 8.4 %copy.172 = bf16[1,16,8192]{1,0,2:T(2,128)(2,1)} copy(bf16[1,16,8192]{2,1,0:T(8,128)(2,1)} %param.12) | data formatting | bytes 524288 | tf_op args[3]
  21.9 45.3 %reduce.1 = bf16[8192,16]{1,0:T(8,128)(2,1)S(1)} reduce(bf16[8192,1,16]{2,1,0:T(2,128)(2,1)} %bitcast.171, bf16[]{:T(256)} %broadcast.69), dimensions={1}, to_apply=%bitcast.141.reduce_sub_computation | reduce | bytes 524290
  67.1 2.8 %reshape.300 = bf16[16,2,4096]{2,1,0:T(2,128)(2,1)} reshape(bf16[8192,16]{1,0:T(8,128)(2,1)S(1)} %reduce.1) | data formatting | bytes 524288
  69.9 9.1 %all-to-all-start.1 = ((bf16[16,2,4096]{2,1,0:T(2,128)(2,1)}), bf16[16,2,4096]{2,1,0:T(2,128)(2,1)S(1)}, u32[]{:S(2)}, u32[]{:S(2)}) async-start(bf16[16,2,4096]{2,1,0:T(2,128)(2,1)} %reshape.300), calls=%async_computation.1 | async-start | bytes 524288 | tf_op jit(solution)/shard_map/all_to_all | solution.py:51
  79.3 6.8 %all-to-all-done.1 = bf16[16,2,4096]{2,1,0:T(2,128)(2,1)S(1)} async-done(((bf16[16,2,4096]{2,1,0:T(2,128)(2,1)}), bf16[16,2,4096]{2,1,0:T(2,128)(2,1)S(1)}, u32[]{:S(2)}, u32[]{:S(2)}) %all-to-all-start.1) | async-done | bytes 262176 | tf_op jit(solution)/shard_map/all_to_all | solution.py:51
  86.1 7.7 %reshape.301 = bf16[8192,1,16]{2,1,0:T(2,128)(2,1)} reshape(bf16[16,2,4096]{2,1,0:T(2,128)(2,1)S(1)} %all-to-all-done.1) | data formatting | bytes 524288
  93.8 7.9 %copy.173 = bf16[1,16,8192]{2,1,0:T(8,128)(2,1)S(1)} copy(bf16[1,16,8192]{1,0,2:T(2,128)(2,1)} %bitcast.172) | data formatting | bytes 524288 | tf_op jit(solution)/shard_map/all_to_all | solution.py:51
  103.2 34.5 %all-gather = f32[32,4,1]{1,2,0:T(1,128)S(1)} all-gather(f32[1,4,1]{1,2,0:T(1,128)S(1)} %get-tuple-element.303), channel_id=2, replica_groups=mesh['ctx'=32,'uly'=16] {'ctx'}, dimensions={0}, use_global_device_ids=true | all-gather | bytes 528 | tf_op jit(solution)/shard_map/all_gather | solution.py:9
  139.7 1.1 convolution_bitcast_fusion.5
  141.1 34.0 %while.28 = (s32[]{:T(128)}, f32[1,4,128,128]{3,2,1,0:T(8,128)S(1)}, s32[]{:T(128)}, f32[32,1,4]{2,1,0:T(1,128)S(1)}, f32[32,1,4,128,128]{4,3,2,1,0:T(8,128)}, /*index=5*/s32[]{:T(128)}, s32[]{:T(128)}) while((s32[]{:T(128)}, f32[1,4,128,128]{3,2,1,0:T(8,128)S(1)}, s32[]{:T(128)}, f32[32,1,4]{2,1,0:T(1,128)S(1)}, ...), condition=%wide.region_3.4_spmd.clone, body=%wide.region_2.3_spmd.clone.sunk | while | flops 262148 | bytes 786585 | solution.py:21
  142.2 1.1 fusion.44
  143.3 1.1 fusion.44
  148.8 1.1 fusion.44
  151.0 1.1 fusion.44
  152.1 1.1 fusion.44
  154.3 1.1 fusion.44
  155.4 1.1 fusion.44
  156.4 1.1 fusion.44
  157.5 1.1 fusion.44
  158.6 1.1 fusion.44
  159.7 1.1 fusion.44
  160.8 1.1 fusion.44
  165.2 1.1 fusion.44
  168.5 1.1 fusion.44
  170.7 1.1 fusion.44
  172.9 1.1 fusion.44
  174.0 1.1 fusion.44
  175.1 1.3 fusion.12
  176.3 1.1 copy.180
  177.5 3.2 %reduce.2 = bf16[256,512]{1,0:T(8,128)(2,1)S(1)} reduce(bf16[256,1,512]{2,1,0:T(2,128)(2,1)} %bitcast.183, bf16[]{:T(256)} %broadcast.69), dimensions={1}, to_apply=%bitcast.143.reduce_sub_computation | reduce | bytes 524290
  181.5 5.1 %all-to-all-start.2 = ((bf16[16,2,4096]{2,1,0:T(2,128)(2,1)}), bf16[16,2,4096]{2,1,0:T(2,128)(2,1)S(1)}, u32[]{:S(2)}, u32[]{:S(2)}) async-start(bf16[16,2,4096]{2,1,0:T(2,128)(2,1)} %reshape.302), calls=%async_computation.2 | async-start | bytes 524288 | tf_op jit(solution)/shard_map/all_to_all | solution.py:113
  187.3 2.3 reduce
  190.5 7.7 %rev.7 = f32[32,1,4,128,128]{4,3,2,1,0:T(8,128)} reverse(f32[32,1,4,128,128]{4,3,2,1,0:T(8,128)} %bitcast.173), dimensions={0} | reverse | bytes 16777216 | tf_op jit(solution)/shard_map/rev | solution.py:11
  198.2 33.8 %while.29 = (s32[]{:T(128)}, f32[1,4,128,128]{3,2,1,0:T(8,128)S(1)}, s32[]{:T(128)}, f32[32,1,4]{2,1,0:T(1,128)S(1)}, f32[32,1,4,128,128]{4,3,2,1,0:T(8,128)}, /*index=5*/s32[]{:T(128)}, s32[]{:T(128)}) while((s32[]{:T(128)}, f32[1,4,128,128]{3,2,1,0:T(8,128)S(1)}, s32[]{:T(128)}, f32[32,1,4]{2,1,0:T(1,128)S(1)}, ...), condition=%wide.region_5.6_spmd.clone, body=%wide.region_4.5_spmd.clone.sunk | while | flops 262148 | bytes 786585 | solution.py:21
  199.3 1.1 fusion.45
  200.4 1.1 fusion.45
  201.5 1.1 fusion.45
  202.6 1.1 fusion.45
  203.7 1.1 fusion.45
  204.7 1.1 fusion.45
  206.9 1.1 fusion.45
  208.0 1.1 fusion.45
  209.1 1.1 fusion.45
  210.2 1.1 fusion.45
  211.3 1.1 fusion.45
  212.4 1.1 fusion.45
  214.6 1.1 fusion.45
  215.7 1.1 fusion.45
  216.8 1.1 fusion.45
  217.9 1.1 fusion.45
  218.9 1.1 fusion.45
  220.0 1.1 fusion.45
  221.1 1.1 fusion.45
  222.2 1.1 fusion.45
  232.0 7.2 %all-to-all-start = ((bf16[16,2,4096]{2,1,0:T(2,128)(2,1)}), bf16[16,2,4096]{2,1,0:T(2,128)(2,1)S(1)}, u32[]{:S(2)}, u32[]{:S(2)}) async-start(bf16[16,2,4096]{2,1,0:T(2,128)(2,1)} %reshape.298), calls=%async_computation | async-start | bytes 524288 | tf_op jit(solution)/shard_map/all_to_all | solution.py:112
  240.0 2.3 reduce.3
  243.1 3.2 %all-to-all-done = bf16[16,2,4096]{2,1,0:T(2,128)(2,1)S(1)} async-done(((bf16[16,2,4096]{2,1,0:T(2,128)(2,1)}), bf16[16,2,4096]{2,1,0:T(2,128)(2,1)S(1)}, u32[]{:S(2)}, u32[]{:S(2)}) %all-to-all-start) | async-done | bytes 262176 | tf_op jit(solution)/shard_map/all_to_all | solution.py:112
  246.3 5.1 %all-to-all-start.3 = ((bf16[16,2,4096]{2,1,0:T(2,128)(2,1)}), bf16[16,2,4096]{2,1,0:T(2,128)(2,1)S(1)}, u32[]{:S(2)}, u32[]{:S(2)}) async-start(bf16[16,2,4096]{2,1,0:T(2,128)(2,1)} %reshape.304), calls=%async_computation.3 | async-start | bytes 524288 | tf_op jit(solution)/shard_map/all_to_all | solution.py:114
  252.2 2.3 reduce.4
  255.3 3.1 %all-to-all-done.3 = bf16[16,2,4096]{2,1,0:T(2,128)(2,1)S(1)} async-done(((bf16[16,2,4096]{2,1,0:T(2,128)(2,1)}), bf16[16,2,4096]{2,1,0:T(2,128)(2,1)S(1)}, u32[]{:S(2)}, u32[]{:S(2)}) %all-to-all-start.3) | async-done | bytes 262176 | tf_op jit(solution)/shard_map/all_to_all | solution.py:114
  258.4 5.2 %all-to-all-start.4 = ((bf16[16,2,4096]{2,1,0:T(2,128)(2,1)}), bf16[16,2,4096]{2,1,0:T(2,128)(2,1)S(1)}, u32[]{:S(2)}, u32[]{:S(2)}) async-start(bf16[16,2,4096]{2,1,0:T(2,128)(2,1)} %reshape.306), calls=%async_computation.4 | async-start | bytes 524288 | tf_op jit(solution)/shard_map/all_to_all | solution.py:115
  266.7 3.9 %all-to-all-done.4 = bf16[16,2,4096]{2,1,0:T(2,128)(2,1)S(1)} async-done(((bf16[16,2,4096]{2,1,0:T(2,128)(2,1)}), bf16[16,2,4096]{2,1,0:T(2,128)(2,1)S(1)}, u32[]{:S(2)}, u32[]{:S(2)}) %all-to-all-start.4) | async-done | bytes 262176 | tf_op jit(solution)/shard_map/all_to_all | solution.py:115
  (155 shorter events, 44.4 us)
Async XLA Ops:
  7.2 133.9 %all-gather.6.cloned.1.call-start = ((), (), s32[]{:S(2)}) async-start(), calls=%async_computation.5 | async-start | bytes 8650752 | tf_op jit(solution)/shard_map/all_gather | solution.py:9
  9.5 69.7 %copy-start = (bf16[1,256,512]{2,1,0:T(8,128)(2,1)S(1)}, bf16[1,256,512]{2,1,0:T(8,128)(2,1)}, u32[]{:S(2)}) copy-start(bf16[1,256,512]{2,1,0:T(8,128)(2,1)} %param.9) | copy-start | bytes 786436
  69.9 16.2 %all-to-all-start.1 = ((bf16[16,2,4096]{2,1,0:T(2,128)(2,1)}), bf16[16,2,4096]{2,1,0:T(2,128)(2,1)S(1)}, u32[]{:S(2)}, u32[]{:S(2)}) async-start(bf16[16,2,4096]{2,1,0:T(2,128)(2,1)} %reshape.300), calls=%async_computation.1 | async-start | bytes 524288 | tf_op jit(solution)/shard_map/all_to_all | solution.py:51
  79.1 111.4 %all-gather.8.cloned.1.call-start = ((), (), s32[]{:S(2)}) async-start(), calls=%async_computation.6 | async-start | bytes 8650752 | tf_op jit(solution)/shard_map/all_gather | solution.py:9
  181.5 50.5 %all-to-all-start.2 = ((bf16[16,2,4096]{2,1,0:T(2,128)(2,1)}), bf16[16,2,4096]{2,1,0:T(2,128)(2,1)S(1)}, u32[]{:S(2)}, u32[]{:S(2)}) async-start(bf16[16,2,4096]{2,1,0:T(2,128)(2,1)} %reshape.302), calls=%async_computation.2 | async-start | bytes 524288 | tf_op jit(solution)/shard_map/all_to_all | solution.py:113
  232.0 14.3 %all-to-all-start = ((bf16[16,2,4096]{2,1,0:T(2,128)(2,1)}), bf16[16,2,4096]{2,1,0:T(2,128)(2,1)S(1)}, u32[]{:S(2)}, u32[]{:S(2)}) async-start(bf16[16,2,4096]{2,1,0:T(2,128)(2,1)} %reshape.298), calls=%async_computation | async-start | bytes 524288 | tf_op jit(solution)/shard_map/all_to_all | solution.py:112
  246.3 12.1 %all-to-all-start.3 = ((bf16[16,2,4096]{2,1,0:T(2,128)(2,1)}), bf16[16,2,4096]{2,1,0:T(2,128)(2,1)S(1)}, u32[]{:S(2)}, u32[]{:S(2)}) async-start(bf16[16,2,4096]{2,1,0:T(2,128)(2,1)} %reshape.304), calls=%async_computation.3 | async-start | bytes 524288 | tf_op jit(solution)/shard_map/all_to_all | solution.py:114
  258.4 12.1 %all-to-all-start.4 = ((bf16[16,2,4096]{2,1,0:T(2,128)(2,1)}), bf16[16,2,4096]{2,1,0:T(2,128)(2,1)S(1)}, u32[]{:S(2)}, u32[]{:S(2)}) async-start(bf16[16,2,4096]{2,1,0:T(2,128)(2,1)} %reshape.306), calls=%async_computation.4 | async-start | bytes 524288 | tf_op jit(solution)/shard_map/all_to_all | solution.py:115
Sparse Core Ops, SparseCore 0:
  13.0 83.9 all-gather.5
  103.3 79.5 all-gather.7
where the time goes:
time: 282 us; the launch traced here: 278 us
  other arithmetic  122 us (43%)
  local copies, waits for them, and re-layouts  50.1 us (18%)
  blocking collectives  34.5 us (12%)
  starting transfers between devices  31.8 us (11%)
  waiting for transfers between devices  17 us (6%)
  between operations  14.4 us (5%)
  matrix products  6.72 us (2%)
    select_n x62, other arithmetic, hop(): jnp.where(position < mine, new, old)  65.4 us
    unnamed x7, other arithmetic  55.2 us
    all_gather x1, blocking collectives, entering(): pieces = jax.tree.map(lambda part: lax.all_gather(part, axis), value)  34.5 us
    unnamed x21, local copies, waits for them, and re-layouts  24.5 us
    all_to_all x1, starting transfers between devices, local(): lax.all_to_all(grad_out, 'uly', split_axis=2, concat_axis=1, tiled=True)  9.14 us
    all_to_all x3, local copies, waits for them, and re-layouts, local(): lax.all_to_all(grad_out, 'uly', split_axis=2, concat_axis=1, tiled=True)  8.03 us
    rev x2, local copies, waits for them, and re-layouts, entering(): pieces = jax.tree.map(lambda part: part[::-1], pieces)  7.8 us
    all_to_all x1, starting transfers between devices, local(): lax.all_to_all(to_tokens(attended), 'uly', split_axis=1, concat_axis=2, t...  7.24 us
  transfers between devices with their start and end apart: 7, of which 4 were waited for; matrix products, arithmetic and copies ran while one was open for 62% of the time, Pallas kernels for 0%

commit v1 on v0

--- a/solution.py
+++ b/solution.py
@@ -110,7 +110,15 @@
 
     attended_rows, query_rows, key_rows, value_rows = (
         lax.all_to_all(to_tokens(attended), "uly", split_axis=1, concat_axis=2, tiled=True),
-        lax.all_to_all(to_tokens(query_part), "uly", split_axis=1, concat_axis=2, tiled=True),
+        jnp.concatenate(
+            lax.all_to_all(
+                jnp.stack(jnp.split(to_tokens(query_part), lax.axis_size("uly"), axis=1)),
+                "uly",
+                0,
+                0,
+            ),
+            axis=2,
+        ),
         lax.all_to_all(to_tokens(key_part), "uly", split_axis=1, concat_axis=2, tiled=True),
         lax.all_to_all(to_tokens(value_part), "uly", split_axis=1, concat_axis=2, tiled=True),
     )

time: 282 us -> 337 us (1.20)
  local copies, waits for them, and re-layouts: 50.1 us -> 108 us
  other arithmetic: 122 us -> 118 us
    unnamed x21 -> x53, local copies, waits for them, and re-layouts: 24.5 us -> 60.5 us
    mul x62, local copies, waits for them, and re-layouts: 0.42 us -> 20 us  [combine(): latter[0][..., None, None] * earlier[1] + latter[1]]
    unnamed x7 -> x6, other arithmetic: 55.2 us -> 51.8 us
  transfers between devices with their start and end apart: 7 -> 7, of which waited for: 4 -> 4; matrix products, arithmetic and copies ran while one was open for 62% -> 68% of each run, Pallas kernels for 0% -> 0%
where the time goes in v1:
time: 337 us; the launch traced here: 333 us
  other arithmetic  118 us (35%)
  local copies, waits for them, and re-layouts  108 us (32%)
  blocking collectives  34.5 us (10%)
  starting transfers between devices  31.7 us (9%)
  waiting for transfers between devices  16.4 us (5%)
  between operations  14.4 us (4%)
  matrix products  7.77 us (2%)
    select_n x62, other arithmetic, hop(): jnp.where(position < mine, new, old)  65.3 us
    unnamed x53, local copies, waits for them, and re-layouts  60.5 us
    unnamed x6, other arithmetic  51.8 us
    all_gather x1, blocking collectives, entering(): pieces = jax.tree.map(lambda part: lax.all_gather(part, axis), value)  34.5 us
    mul x62, local copies, waits for them, and re-layouts, combine(): latter[0][..., None, None] * earlier[1] + latter[1]  20 us
    all_to_all x1, starting transfers between devices, local(): lax.all_to_all(grad_out, 'uly', split_axis=2, concat_axis=1, tiled=True)  9.14 us
    all_to_all x3, local copies, waits for them, and re-layouts, local(): lax.all_to_all(grad_out, 'uly', split_axis=2, concat_axis=1, tiled=True)  8.05 us
    rev x2, local copies, waits for them, and re-layouts, entering(): pieces = jax.tree.map(lambda part: part[::-1], pieces)  7.81 us
  transfers between devices with their start and end apart: 7, of which 4 were waited for; matrix products, arithmetic and copies ran while one was open for 68% of the time, Pallas kernels for 0%

profile of v1, /device:TPU:8, one launch (start us, length us, event | category | flops | bytes accessed | tf_op | source)
XLA Modules:
  0.0 332.6 jit_solution(12000075276087398447)
XLA Ops:
  7.9 1.2 reduce-window.6
  9.6 1.1 reshape.285
  12.9 8.4 %copy.185 = bf16[1,16,8192]{1,0,2:T(2,128)(2,1)} copy(bf16[1,16,8192]{2,1,0:T(8,128)(2,1)} %param.12) | data formatting | bytes 524288 | tf_op args[3]
  21.8 45.2 %reduce.1 = bf16[8192,16]{1,0:T(8,128)(2,1)S(1)} reduce(bf16[8192,1,16]{2,1,0:T(2,128)(2,1)} %bitcast.200, bf16[]{:T(256)} %broadcast.69), dimensions={1}, to_apply=%bitcast.171.reduce_sub_computation | reduce | bytes 524290
  67.0 2.8 reshape.308
  69.8 9.1 %all-to-all-start.1 = ((bf16[16,2,4096]{2,1,0:T(2,128)(2,1)}), bf16[16,2,4096]{2,1,0:T(2,128)(2,1)S(1)}, u32[]{:S(2)}, u32[]{:S(2)}) async-start(bf16[16,2,4096]{2,1,0:T(2,128)(2,1)} %reshape.308), calls=%async_computation.1 | async-start | bytes 524288 | tf_op jit(solution)/shard_map/all_to_all | solution.py:51
  79.3 6.6 %all-to-all-done.1 = bf16[16,2,4096]{2,1,0:T(2,128)(2,1)S(1)} async-done(((bf16[16,2,4096]{2,1,0:T(2,128)(2,1)}), bf16[16,2,4096]{2,1,0:T(2,128)(2,1)S(1)}, u32[]{:S(2)}, u32[]{:S(2)}) %all-to-all-start.1) | async-done | bytes 262176 | tf_op jit(solution)/shard_map/all_to_all | solution.py:51
  86.0 7.6 %reshape.309 = bf16[8192,1,16]{2,1,0:T(2,128)(2,1)} reshape(bf16[16,2,4096]{2,1,0:T(2,128)(2,1)S(1)} %all-to-all-done.1) | data formatting | bytes 524288
  93.6 7.9 %copy.186 = bf16[1,16,8192]{2,1,0:T(8,128)(2,1)S(1)} copy(bf16[1,16,8192]{1,0,2:T(2,128)(2,1)} %bitcast.201) | data formatting | bytes 524288 | tf_op jit(solution)/shard_map/all_to_all | solution.py:51
  103.4 34.5 %all-gather = f32[32,4,1]{1,2,0:T(1,128)S(1)} all-gather(f32[1,4,1]{1,2,0:T(1,128)S(1)} %get-tuple-element.319), channel_id=2, replica_groups=mesh['ctx'=32,'uly'=16] {'ctx'}, dimensions={0}, use_global_device_ids=true | all-gather | bytes 528 | tf_op jit(solution)/shard_map/all_gather | solution.py:9
  139.7 1.1 convolution_bitcast_fusion.5
  141.0 1.3 convolution_bitcast_fusion
  142.3 34.0 %while.28 = (s32[]{:T(128)}, f32[1,4,128,128]{3,2,1,0:T(8,128)S(1)}, s32[]{:T(128)}, f32[32,1,4]{2,1,0:T(1,128)S(1)}, f32[32,1,4,128,128]{4,3,2,1,0:T(8,128)}, /*index=5*/s32[]{:T(128)}, s32[]{:T(128)}) while((s32[]{:T(128)}, f32[1,4,128,128]{3,2,1,0:T(8,128)S(1)}, s32[]{:T(128)}, f32[32,1,4]{2,1,0:T(1,128)S(1)}, ...), condition=%wide.region_3.4_spmd.clone, body=%wide.region_2.3_spmd.clone.sunk | while | flops 262148 | bytes 786585 | solution.py:21
  142.3 1.1 fusion.45
  144.5 1.1 fusion.45
  146.7 1.1 fusion.45
  147.8 1.1 fusion.45
  151.1 1.1 fusion.45
  152.2 1.1 fusion.45
  156.6 1.1 fusion.45
  164.3 1.1 fusion.45
  165.4 1.1 fusion.45
  168.6 1.1 fusion.45
  170.8 1.1 fusion.45
  171.9 1.1 fusion.45
  175.2 1.1 fusion.45
  176.3 1.3 fusion.12
  177.6 1.7 fusion.31
  179.3 1.6 copy.231
  180.8 1.6 copy.232
  182.4 1.6 copy.233
  184.0 1.6 copy.234
  185.6 1.6 copy.235
  187.1 1.6 copy.236
  188.7 1.6 copy.237
  190.3 1.6 copy.238
  191.9 1.6 copy.239
  193.5 1.6 copy.240
  195.0 1.6 copy.241
  197.7 1.3 constant_dynamic-update-slice_fusion.15
  199.0 1.3 constant_dynamic-update-slice_fusion.14
  200.3 1.3 constant_dynamic-update-slice_fusion.13
  201.6 1.3 constant_dynamic-update-slice_fusion.12
  203.0 1.3 constant_dynamic-update-slice_fusion.11
  204.3 1.3 constant_dynamic-update-slice_fusion.10
  205.6 1.3 constant_dynamic-update-slice_fusion.9
  206.9 1.3 constant_dynamic-update-slice_fusion.8
  208.3 1.3 constant_dynamic-update-slice_fusion.7
  209.6 1.3 constant_dynamic-update-slice_fusion.6
  210.9 1.3 constant_dynamic-update-slice_fusion.5
  212.2 1.3 constant_dynamic-update-slice_fusion.4
  216.0 5.1 %all-to-all-start.2 = ((bf16[16,1,16,512]{3,2,1,0:T(8,128)(2,1)}), bf16[16,1,16,512]{3,2,1,0:T(8,128)(2,1)S(1)}, u32[]{:S(2)}, u32[]{:S(2)}) async-start(bf16[16,1,16,512]{3,2,1,0:T(8,128)(2,1)} %constant_dynamic-update-slice_fusion), calls=%async_computation.2 | async-start | bytes 524288 | tf_op jit(solution)/shard_map/all_to_all | solution.py:114
  221.8 2.2 reduce
  224.9 7.7 %rev.7 = f32[32,1,4,128,128]{4,3,2,1,0:T(8,128)} reverse(f32[32,1,4,128,128]{4,3,2,1,0:T(8,128)} %bitcast.202), dimensions={0} | reverse | bytes 16777216 | tf_op jit(solution)/shard_map/rev | solution.py:11
  232.6 52.9 %while.29 = (s32[]{:T(128)}, f32[1,4,128,128]{3,2,1,0:T(8,128)S(1)}, s32[]{:T(128)}, f32[32,1,4]{2,1,0:T(1,128)}, f32[32,1,4,128,128]{4,3,2,1,0:T(8,128)}, /*index=5*/s32[]{:T(128)}, s32[]{:T(128)}) while((s32[]{:T(128)}, f32[1,4,128,128]{3,2,1,0:T(8,128)S(1)}, s32[]{:T(128)}, f32[32,1,4]{2,1,0:T(1,128)}, ...), condition=%wide.region_5.6_spmd.clone, body=%wide.region_4.5_spmd.clone.sunk | while | flops 262148 | bytes 786585 | solution.py:21
  286.2 7.2 %all-to-all-start = ((bf16[16,2,4096]{2,1,0:T(2,128)(2,1)}), bf16[16,2,4096]{2,1,0:T(2,128)(2,1)S(1)}, u32[]{:S(2)}, u32[]{:S(2)}) async-start(bf16[16,2,4096]{2,1,0:T(2,128)(2,1)} %reshape.306), calls=%async_computation | async-start | bytes 524288 | tf_op jit(solution)/shard_map/all_to_all | solution.py:112
  294.1 2.2 reduce.2
  297.2 3.3 all-to-all-done
  300.5 5.1 %all-to-all-start.3 = ((bf16[16,2,4096]{2,1,0:T(2,128)(2,1)}), bf16[16,2,4096]{2,1,0:T(2,128)(2,1)S(1)}, u32[]{:S(2)}, u32[]{:S(2)}) async-start(bf16[16,2,4096]{2,1,0:T(2,128)(2,1)} %reshape.310), calls=%async_computation.3 | async-start | bytes 524288 | tf_op jit(solution)/shard_map/all_to_all | solution.py:122
  306.3 2.2 reduce.3
  309.4 3.2 all-to-all-done.3
  312.6 5.2 %all-to-all-start.4 = ((bf16[16,2,4096]{2,1,0:T(2,128)(2,1)}), bf16[16,2,4096]{2,1,0:T(2,128)(2,1)S(1)}, u32[]{:S(2)}, u32[]{:S(2)}) async-start(bf16[16,2,4096]{2,1,0:T(2,128)(2,1)} %reshape.312), calls=%async_computation.4 | async-start | bytes 524288 | tf_op jit(solution)/shard_map/all_to_all | solution.py:123
  317.7 1.7 copy.249
  321.5 3.2 all-to-all-done.4
  (187 shorter events, 91.7 us)
Async XLA Ops:
  7.2 135.1 %all-gather.6.cloned.1.call-start = ((), (), s32[]{:S(2)}) async-start(), calls=%async_computation.5 | async-start | bytes 8650752 | tf_op jit(solution)/shard_map/all_gather | solution.py:9
  9.6 69.5 %copy-start.2 = (bf16[1,256,512]{2,1,0:T(8,128)(2,1)S(1)}, bf16[1,256,512]{2,1,0:T(8,128)(2,1)}, u32[]{:S(2)}) copy-start(bf16[1,256,512]{2,1,0:T(8,128)(2,1)} %param.9) | copy-start | bytes 786436
  69.8 16.2 %all-to-all-start.1 = ((bf16[16,2,4096]{2,1,0:T(2,128)(2,1)}), bf16[16,2,4096]{2,1,0:T(2,128)(2,1)S(1)}, u32[]{:S(2)}, u32[]{:S(2)}) async-start(bf16[16,2,4096]{2,1,0:T(2,128)(2,1)} %reshape.308), calls=%async_computation.1 | async-start | bytes 524288 | tf_op jit(solution)/shard_map/all_to_all | solution.py:51
  78.9 145.9 %all-gather.8.cloned.1.call-start = ((), (), s32[]{:S(2)}) async-start(), calls=%async_computation.6 | async-start | bytes 8650752 | tf_op jit(solution)/shard_map/all_gather | solution.py:9
  103.4 37.4 %copy-start = (bf16[4,256,256]{2,1,0:T(8,128)(2,1)}, bf16[4,256,256]{2,1,0:T(8,128)(2,1)S(1)}, u32[]{:S(2)}) copy-start(bf16[4,256,256]{2,1,0:T(8,128)(2,1)S(1)} %fusion.2) | copy-start | bytes 1572868
  216.0 69.5 %all-to-all-start.2 = ((bf16[16,1,16,512]{3,2,1,0:T(8,128)(2,1)}), bf16[16,1,16,512]{3,2,1,0:T(8,128)(2,1)S(1)}, u32[]{:S(2)}, u32[]{:S(2)}) async-start(bf16[16,1,16,512]{3,2,1,0:T(8,128)(2,1)} %constant_dynamic-update-slice_fusion), calls=%async_computation.2 | async-start | bytes 524288 | tf_op jit(solution)/shard_map/all_to_all | solution.py:114
  285.5 0.7 copy-start.1
  286.2 14.3 %all-to-all-start = ((bf16[16,2,4096]{2,1,0:T(2,128)(2,1)}), bf16[16,2,4096]{2,1,0:T(2,128)(2,1)S(1)}, u32[]{:S(2)}, u32[]{:S(2)}) async-start(bf16[16,2,4096]{2,1,0:T(2,128)(2,1)} %reshape.306), calls=%async_computation | async-start | bytes 524288 | tf_op jit(solution)/shard_map/all_to_all | solution.py:112
  300.5 12.0 %all-to-all-start.3 = ((bf16[16,2,4096]{2,1,0:T(2,128)(2,1)}), bf16[16,2,4096]{2,1,0:T(2,128)(2,1)S(1)}, u32[]{:S(2)}, u32[]{:S(2)}) async-start(bf16[16,2,4096]{2,1,0:T(2,128)(2,1)} %reshape.310), calls=%async_computation.3 | async-start | bytes 524288 | tf_op jit(solution)/shard_map/all_to_all | solution.py:122
  312.6 12.1 %all-to-all-start.4 = ((bf16[16,2,4096]{2,1,0:T(2,128)(2,1)}), bf16[16,2,4096]{2,1,0:T(2,128)(2,1)S(1)}, u32[]{:S(2)}, u32[]{:S(2)}) async-start(bf16[16,2,4096]{2,1,0:T(2,128)(2,1)} %reshape.312), calls=%async_computation.4 | async-start | bytes 524288 | tf_op jit(solution)/shard_map/all_to_all | solution.py:123
Sparse Core Ops, SparseCore 0:
  13.0 83.9 all-gather.5
  103.1 79.9 all-gather.7
